TPU v7x, 512 devices: a whole 4x8x8 slice. The times are simulated.
512 devices in a mesh: fsdp: 128 (over y, z, core), tensor: 4 (over x).
Axes of the slice: x: 4, y: 8, z: 8, core: 2. Of those that a mesh axis runs over, the one named last changes fastest.
Arguments:
- layer_inputs: bfloat16 [2, 49152, 5120], P(None, 'fsdp', 'tensor'), may hold values from -8 to 8, as said below
- out_grads: bfloat16 [2, 49152, 2560], P(None, 'fsdp', 'tensor'), may hold values from -8 to 8, as said below
- weight_grad: bfloat16 [2, 2560, 5120], P(None, 'fsdp', 'tensor'), may hold values from -0.059814453 to 0.059814453
- emb_grad: bfloat16 [50176, 2560], P('fsdp', 'tensor'), may hold values from -0.59765625 to 0.59765625
- counts: int32 [50176], P('fsdp'), may hold values from 0 to 250
- owner_pos: int32 [4, 30], P('tensor'), may hold values from 0 to 127, as said below
Outputs:
- update: bfloat16 [2, 2560, 5120], P(None, 'fsdp', 'tensor')
- owner_inverses: float32 [4, 128, 128, 128], P('tensor', 'fsdp')
- emb_update: bfloat16 [50176, 2560], P('fsdp', 'tensor')
Inputs may be any that keep to these rules, and one draw needn't show every extreme that they name: `layer_inputs`: every element lies within the stated range; inner units in groups of four share a common part. `out_grads`: every element lies within the stated range; features in groups of four share a common part. `owner_pos`: the 30 entries of a row are distinct; slot p belongs to fsdp index p; some fsdp index holds 1 block of each row.
All inputs are finite; a program needn't handle non-finite values. Where the computation divides by a largest or mean magnitude, that divisor is 1e-20 or more.
Results may differ from a plain program's by a relative error of at most 0.0062.
Values may be sent and summed in bfloat16 or wider, within the bound.
No kernel may reach another device: no remote copies, remote signals or barrier semaphores. Data moves between devices by JAX's collectives and lax.ppermute only.
A program may use at most 64 MiB of HBM per device.

v0:
```python
import jax
import jax.numpy as jnp
from jax import lax
from jax.sharding import PartitionSpec as P

BLK = 128
NS_ITERS = 8
DAMP = 0.02
EDAMP = 0.25


def newton_inverse(factor):
    identity = jnp.eye(factor.shape[-1], dtype=jnp.float32)
    damped = factor + DAMP * identity
    norm_scale = jnp.max(jnp.sum(jnp.abs(damped), axis=-1), axis=-1)
    approx = identity[None] / norm_scale[:, None, None]
    for sweep_idx in range(NS_ITERS):
        product = jnp.einsum("bij,bjk->bik", damped, approx, precision=lax.Precision.HIGHEST)
        approx = jnp.einsum(
            "bij,bjk->bik", approx, 2.0 * identity[None] - product, precision=lax.Precision.HIGHEST
        )
    return approx


def on_device(layer_inputs, out_grads, weight_grad, emb_grad, counts, owner_pos):
    fsdp_size = lax.axis_size("fsdp")
    layers, row_count, inner_local = layer_inputs.shape
    width_local = out_grads.shape[2]
    a_count = inner_local // BLK
    g_count = width_local // BLK
    input_blocks = layer_inputs.reshape(layers, row_count, a_count, BLK)
    a_part = jnp.einsum(
        "lrbi,lrbj->lbij", input_blocks, input_blocks, preferred_element_type=jnp.float32
    )
    grad_blocks = out_grads.reshape(layers, row_count, g_count, BLK)
    g_part = jnp.einsum(
        "lrbi,lrbj->lbij", grad_blocks, grad_blocks, preferred_element_type=jnp.float32
    )
    partials = jnp.concatenate([a_part, g_part], axis=1)
    count_part = jnp.sum(counts.astype(jnp.float32))
    block_total = layers * (a_count + g_count)
    own_table = owner_pos[0]
    slot_count = (block_total + fsdp_size - 1) // fsdp_size
    wanted = lax.axis_index("fsdp") * slot_count + jnp.arange(slot_count, dtype=jnp.int32)
    one_hot = (own_table[None, :] == wanted[:, None]).astype(jnp.float32)
    divisor = row_count * fsdp_size
    summed, count_total = lax.psum((partials, count_part), "fsdp")
    factors = (summed / divisor).reshape(-1, BLK, BLK)
    mine_blocks = jnp.einsum("sk,kij->sij", one_hot, factors, precision=lax.Precision.HIGHEST)
    held_inv = newton_inverse(mine_blocks) * jnp.max(one_hot, axis=1)[:, None, None]
    owner_out = held_inv[None]
    shared = lax.all_gather(held_inv.astype(jnp.bfloat16), "fsdp", axis=0, tiled=True)
    low_inv = jnp.take(shared, own_table, axis=0)
    low_inv = low_inv.reshape(layers, a_count + g_count, BLK, BLK)
    a_low = low_inv[:, :a_count]
    g_own = low_inv[:, a_count:]
    g_all = lax.all_gather(g_own, "tensor", axis=1, tiled=True)
    d_local = weight_grad.shape[1]
    grad_split = weight_grad.reshape(layers, d_local, a_count, BLK)
    right_done = jnp.einsum(
        "ldbi,lbij->ldbj", grad_split, a_low, preferred_element_type=jnp.float32
    )
    right_done = right_done.reshape(layers, d_local, inner_local).astype(jnp.bfloat16)
    columns = lax.all_to_all(right_done, "fsdp", split_axis=2, concat_axis=1, tiled=True)
    full_width = columns.shape[1]
    column_blocks = columns.reshape(layers, full_width // BLK, BLK, columns.shape[2])
    left_done = jnp.einsum(
        "lbij,lbjc->lbic", g_all, column_blocks, preferred_element_type=jnp.float32
    )
    left_done = left_done.reshape(columns.shape).astype(jnp.bfloat16)
    update = lax.all_to_all(left_done, "fsdp", split_axis=1, concat_axis=2, tiled=True)
    vocab_total = counts.shape[0] * fsdp_size
    frequency = counts.astype(jnp.float32) * vocab_total / count_total
    emb_update = (emb_grad.astype(jnp.float32) / (frequency + EDAMP)[:, None]).astype(jnp.bfloat16)
    return (update, owner_out, emb_update)


def solution(mesh):
    placed = (
        P(None, "fsdp", "tensor"),
        P(None, "fsdp", "tensor"),
        P(None, "fsdp", "tensor"),
        P("fsdp", "tensor"),
        P("fsdp"),
        P("tensor", None),
    )
    return jax.shard_map(
        on_device,
        mesh=mesh,
        in_specs=placed,
        out_specs=(P(None, "fsdp", "tensor"), P("tensor", "fsdp", None, None), P("fsdp", "tensor")),
        check_vma=False,
    )
```

profile of v0, /device:TPU:1, one launch (start us, length us, event | category | flops | bytes accessed | tf_op | source)
XLA Modules:
  0.0 627.3 jit_solution(3849056643370400006)
XLA Ops:
  7.2 2.8 copy.41
  10.1 0.9 fusion.20
  11.0 1.6 copy.43
  13.1 1.4 pad_maximum_fusion
  15.2 0.6 fusion.14
  15.8 206.1 %all-reduce.2.cloned.1.call-done = f32[2,15,128,128]{3,2,1,0:T(8,128)} async-done(((f32[2,15,128,128]{3,2,1,0:T(8,128)}), f32[2,15,128,128]{3,2,1,0:T(8,128)}) %all-reduce.2.cloned.1.call-update) | async-done | bytes 1966096 | tf_op jit(solution)/shard_map/psum | solution.py:47
  221.9 1.7 broadcast_multiply_fusion
  223.6 1.9 fusion
  225.6 0.6 reduce_max.18
  230.1 1.5 fusion.19
  232.2 0.7 reduce.8
  232.9 81.3 %all-gather.6.cloned.1.call-done = bf16[16384,128]{1,0:T(8,128)(2,1)} async-done(((bf16[128,128]{1,0:T(8,128)(2,1)}), bf16[16384,128]{1,0:T(8,128)(2,1)}) %all-gather.6.cloned.1.call-update) | async-done | bytes 4194320 | tf_op jit(solution)/shard_map/all_gather | solution.py:52
  314.3 2.9 gather_fusion
  317.4 0.7 slice.10
  318.2 0.6 convert_reduce_fusion
  318.8 247.1 %psum.15 = f32[]{:T(128)} all-reduce(f32[]{:T(128)} %convert_reduce_fusion), channel_id=1, replica_groups=mesh['fsdp'=128,'tensor'=4] {'fsdp'}, use_global_device_ids=true, to_apply=%region_5.0 | all-reduce | flops 1 | bytes 8 | tf_op jit(solution)/shard_map/psum | solution.py:47
  566.7 1.2 reshape.204
  567.9 10.2 %all-to-all-start = ((bf16[128,2,200]{2,1,0:T(2,128)(2,1)}), bf16[128,2,200]{2,1,0:T(2,128)(2,1)S(1)}, u32[]{:S(2)}, u32[]{:S(2)}) async-start(bf16[128,2,200]{2,1,0:T(2,128)(2,1)} %reshape.204), calls=%async_computation | async-start | bytes 262144 | tf_op jit(solution)/shard_map/all_to_all | solution.py:64
  578.1 0.7 divide_add_fusion
  578.7 11.6 %all-to-all-done = bf16[128,2,200]{2,1,0:T(2,128)(2,1)S(1)} async-done(((bf16[128,2,200]{2,1,0:T(2,128)(2,1)}), bf16[128,2,200]{2,1,0:T(2,128)(2,1)S(1)}, u32[]{:S(2)}, u32[]{:S(2)}) %all-to-all-start) | async-done | bytes 102432 | tf_op jit(solution)/shard_map/all_to_all | solution.py:64
  590.3 0.6 reshape.205
  591.1 1.4 reshape.183
  592.5 2.1 convolution_convert_fusion
  594.5 1.1 copy.60
  595.6 1.6 reshape.206
  597.2 6.1 all-to-all-start.1
  603.4 1.0 divide_convert_fusion
  604.3 11.4 %all-to-all-done.1 = bf16[128,2,200]{2,1,0:T(2,128)(2,1)S(1)} async-done(((bf16[128,2,200]{2,1,0:T(2,128)(2,1)}), bf16[128,2,200]{2,1,0:T(2,128)(2,1)S(1)}, u32[]{:S(2)}, u32[]{:S(2)}) %all-to-all-start.1) | async-done | bytes 102432 | tf_op jit(solution)/shard_map/all_to_all | solution.py:71
  615.7 1.0 reshape.207
  616.7 2.3 copy.61
  619.0 0.7 copy.53
  619.7 1.1 copy.54
  (42 shorter events, 6.3 us)
Async XLA Ops:
  7.2 214.7 %all-reduce.2.cloned.1.call-start = ((), (), s32[]{:S(2)}) async-start(), calls=%async_computation.2 | async-start | bytes 3932160 | tf_op jit(solution)/shard_map/psum | solution.py:47
  14.6 0.7 copy-start.3
  14.6 299.7 %all-gather.6.cloned.1.call-start = ((), (), s32[]{:S(2)}) async-start(), calls=%async_computation.4 | async-start | bytes 4227072 | tf_op jit(solution)/shard_map/all_gather | solution.py:52
  231.6 360.8 %all-gather.4.cloned.1.call-start = ((), (), s32[]{:S(2)}) async-start(), calls=%async_computation.3 | async-start | bytes 1638400 | tf_op jit(solution)/shard_map/all_gather | solution.py:57
  317.2 1.0 copy-start.2
  317.2 248.6 %copy-start.1 = (bf16[2,20,1280]{2,0,1:T(2,128)(2,1)S(1)}, bf16[2,20,1280]{2,0,1:T(2,128)(2,1)}, u32[]{:S(2)}) copy-start(bf16[2,20,1280]{2,0,1:T(2,128)(2,1)} %param.8) | copy-start | bytes 307204
  567.9 22.4 %all-to-all-start = ((bf16[128,2,200]{2,1,0:T(2,128)(2,1)}), bf16[128,2,200]{2,1,0:T(2,128)(2,1)S(1)}, u32[]{:S(2)}, u32[]{:S(2)}) async-start(bf16[128,2,200]{2,1,0:T(2,128)(2,1)} %reshape.204), calls=%async_computation | async-start | bytes 262144 | tf_op jit(solution)/shard_map/all_to_all | solution.py:64
  594.5 8.8 %copy-start = (bf16[392,640]{1,0:T(8,128)(2,1)S(1)}, bf16[392,640]{1,0:T(8,128)(2,1)}, u32[]{:S(2)}) copy-start(bf16[392,640]{1,0:T(8,128)(2,1)} %param.9) | copy-start | bytes 1505284
  597.2 18.5 %all-to-all-start.1 = ((bf16[128,2,200]{2,1,0:T(2,128)(2,1)}), bf16[128,2,200]{2,1,0:T(2,128)(2,1)S(1)}, u32[]{:S(2)}, u32[]{:S(2)}) async-start(bf16[128,2,200]{2,1,0:T(2,128)(2,1)} %reshape.206), calls=%async_computation.1 | async-start | bytes 262144 | tf_op jit(solution)/shard_map/all_to_all | solution.py:71
Sparse Core Ops, SparseCore 0:
  14.7 207.1 all-reduce.1
  231.7 82.4 all-gather.5
  318.3 25.3 all-gather.3
where the time goes:
time: 628 us; the launch traced here: 627 us
  waiting for transfers between devices  310 us (49%)
  blocking collectives  247 us (39%)
  local copies, waits for them, and re-layouts  20.9 us (3%)
  starting transfers between devices  16.4 us (3%)
  between operations  14.8 us (2%)
  matrix products  10.3 us (2%)
  other arithmetic  7.5 us (1%)
    psum x1, blocking collectives, on_device(): summed, count_total = lax.psum((partials, count_part), 'fsdp')  247 us
    psum x1, waiting for transfers between devices, on_device(): summed, count_total = lax.psum((partials, count_part), 'fsdp')  206 us
    all_gather x1, waiting for transfers between devices, on_device(): lax.all_gather(held_inv.astype(jnp.bfloat16), 'fsdp', axis=0, tiled=True)  81.3 us
  transfers between devices with their start and end apart: 5, of which 4 were waited for; matrix products, arithmetic and copies ran while one was open for 1% of the time, Pallas kernels for 0%

commit v1 on v0

--- a/solution.py
+++ b/solution.py
@@ -49,7 +49,12 @@
     mine_blocks = jnp.einsum("sk,kij->sij", one_hot, factors, precision=lax.Precision.HIGHEST)
     held_inv = newton_inverse(mine_blocks) * jnp.max(one_hot, axis=1)[:, None, None]
     owner_out = held_inv[None]
-    shared = lax.all_gather(held_inv.astype(jnp.bfloat16), "fsdp", axis=0, tiled=True)
+    shared = jnp.concatenate(
+        lax.all_to_all(
+            jnp.stack([held_inv.astype(jnp.bfloat16)] * lax.axis_size("fsdp")), "fsdp", 0, 0
+        ),
+        axis=0,
+    )
     low_inv = jnp.take(shared, own_table, axis=0)
     low_inv = low_inv.reshape(layers, a_count + g_count, BLK, BLK)
     a_low = low_inv[:, :a_count]

time: 628 us -> 660 us (1.051)
  starting transfers between devices: 16.4 us -> 30.9 us
  waiting for transfers between devices: 310 us -> 323 us
    all_to_all x0 -> x1, waiting for transfers between devices: none -> 94 us  [on_device(): lax.all_to_all(jnp.stack([held_inv.astype(jnp.bfloat16)] * lax.axis_size(...]
    all_gather x1 -> x0, waiting for transfers between devices: 81.3 us -> none  [on_device(): lax.all_gather(held_inv.astype(jnp.bfloat16), 'fsdp', axis=0, tiled=True)]
    all_to_all x0 -> x1, starting transfers between devices: none -> 11.1 us  [on_device(): lax.all_to_all(jnp.stack([held_inv.astype(jnp.bfloat16)] * lax.axis_size(...]
where the time goes in v1:
time: 660 us; the launch traced here: 659 us
  waiting for transfers between devices  323 us (49%)
  blocking collectives  248 us (38%)
  starting transfers between devices  30.9 us (5%)
  local copies, waits for them, and re-layouts  23.9 us (4%)
  between operations  15.1 us (2%)
  matrix products  10.3 us (2%)
  other arithmetic  7.5 us (1%)
    psum x1, blocking collectives, on_device(): summed, count_total = lax.psum((partials, count_part), 'fsdp')  248 us
    psum x1, waiting for transfers between devices, on_device(): summed, count_total = lax.psum((partials, count_part), 'fsdp')  206 us
    all_to_all x1, waiting for transfers between devices, on_device(): lax.all_to_all(jnp.stack([held_inv.astype(jnp.bfloat16)] * lax.axis_size(...  94 us
    all_to_all x1, starting transfers between devices, on_device(): lax.all_to_all(right_done, 'fsdp', split_axis=2, concat_axis=1, tiled=True)  13.5 us
  transfers between devices with their start and end apart: 5, of which 4 were waited for; matrix products, arithmetic and copies ran while one was open for 1% of the time, Pallas kernels for 0%

profile of v1, /device:TPU:1, one launch (start us, length us, event | category | flops | bytes accessed | tf_op | source)
XLA Modules:
  0.0 659.2 jit_solution(9022765847620277455)
XLA Ops:
  7.2 2.8 copy.41
  10.1 0.9 fusion.20
  11.0 1.6 copy.43
  13.1 1.4 pad_maximum_fusion
  14.6 0.6 copy-done.3
  15.8 206.1 %all-reduce.2.cloned.1.call-done = f32[2,15,128,128]{3,2,1,0:T(8,128)} async-done(((f32[2,15,128,128]{3,2,1,0:T(8,128)}), f32[2,15,128,128]{3,2,1,0:T(8,128)}) %all-reduce.2.cloned.1.call-update) | async-done | bytes 1966096 | tf_op jit(solution)/shard_map/psum | solution.py:47
  221.9 1.7 broadcast_multiply_fusion
  223.6 1.9 fusion
  225.6 0.6 reduce_max.18
  230.1 1.5 fusion.19
  231.6 3.0 stack.2
  234.6 11.1 %all-to-all-start = ((bf16[128,1,128,128]{3,2,1,0:T(8,128)(2,1)}), bf16[128,1,128,128]{3,2,1,0:T(8,128)(2,1)}, u32[]{:S(2)}, u32[]{:S(2)}) async-start(bf16[128,1,128,128]{3,2,1,0:T(8,128)(2,1)} %stack.2), calls=%async_computation | async-start | bytes 8388608 | tf_op jit(solution)/shard_map/all_to_all | solution.py:53
  246.3 0.7 reduce.8
  247.1 94.0 %all-to-all-done = bf16[128,1,128,128]{3,2,1,0:T(8,128)(2,1)} async-done(((bf16[128,1,128,128]{3,2,1,0:T(8,128)(2,1)}), bf16[128,1,128,128]{3,2,1,0:T(8,128)(2,1)}, u32[]{:S(2)}, u32[]{:S(2)}) %all-to-all-start) | async-done | bytes 4194336 | tf_op jit(solution)/shard_map/all_to_all | solution.py:53
  341.1 2.9 gather_fusion
  344.2 0.7 slice.10
  345.6 248.4 %psum.15 = f32[]{:T(128)} all-reduce(f32[]{:T(128)} %convert_reduce_fusion), channel_id=1, replica_groups=mesh['fsdp'=128,'tensor'=4] {'fsdp'}, use_global_device_ids=true, to_apply=%region_5.0 | all-reduce | flops 1 | bytes 8 | tf_op jit(solution)/shard_map/psum | solution.py:47
  594.9 1.2 reshape.210
  596.1 13.5 %all-to-all-start.1 = ((bf16[128,2,200]{2,1,0:T(2,128)(2,1)}), bf16[128,2,200]{2,1,0:T(2,128)(2,1)S(1)}, u32[]{:S(2)}, u32[]{:S(2)}) async-start(bf16[128,2,200]{2,1,0:T(2,128)(2,1)} %reshape.210), calls=%async_computation.1 | async-start | bytes 262144 | tf_op jit(solution)/shard_map/all_to_all | solution.py:69
  609.6 0.7 divide_add_fusion
  610.3 11.6 %all-to-all-done.1 = bf16[128,2,200]{2,1,0:T(2,128)(2,1)S(1)} async-done(((bf16[128,2,200]{2,1,0:T(2,128)(2,1)}), bf16[128,2,200]{2,1,0:T(2,128)(2,1)S(1)}, u32[]{:S(2)}, u32[]{:S(2)}) %all-to-all-start.1) | async-done | bytes 102432 | tf_op jit(solution)/shard_map/all_to_all | solution.py:69
  622.6 1.4 reshape.190
  624.0 2.1 convolution_convert_fusion
  626.1 1.1 copy.60
  627.2 1.6 reshape.212
  628.8 6.1 all-to-all-start.2
  634.9 1.0 divide_convert_fusion
  635.9 11.4 %all-to-all-done.2 = bf16[128,2,200]{2,1,0:T(2,128)(2,1)S(1)} async-done(((bf16[128,2,200]{2,1,0:T(2,128)(2,1)}), bf16[128,2,200]{2,1,0:T(2,128)(2,1)S(1)}, u32[]{:S(2)}, u32[]{:S(2)}) %all-to-all-start.2) | async-done | bytes 102432 | tf_op jit(solution)/shard_map/all_to_all | solution.py:76
  647.3 1.0 reshape.213
  648.3 2.3 copy.61
  650.6 0.7 copy.53
  651.3 1.1 copy.54
  (42 shorter events, 7.4 us)
Async XLA Ops:
  7.2 214.7 %all-reduce.2.cloned.1.call-start = ((), (), s32[]{:S(2)}) async-start(), calls=%async_computation.3 | async-start | bytes 3932160 | tf_op jit(solution)/shard_map/psum | solution.py:47
  14.6 0.7 copy-start.3
  234.6 106.5 %all-to-all-start = ((bf16[128,1,128,128]{3,2,1,0:T(8,128)(2,1)}), bf16[128,1,128,128]{3,2,1,0:T(8,128)(2,1)}, u32[]{:S(2)}, u32[]{:S(2)}) async-start(bf16[128,1,128,128]{3,2,1,0:T(8,128)(2,1)} %stack.2), calls=%async_computation | async-start | bytes 8388608 | tf_op jit(solution)/shard_map/all_to_all | solution.py:53
  245.7 378.3 %all-gather.2.cloned.1.call-start = ((), (), s32[]{:S(2)}) async-start(), calls=%async_computation.4 | async-start | bytes 1638400 | tf_op jit(solution)/shard_map/all_gather | solution.py:62
  344.0 1.0 copy-start.2
  344.0 250.0 %copy-start.1 = (bf16[2,20,1280]{2,0,1:T(2,128)(2,1)S(1)}, bf16[2,20,1280]{2,0,1:T(2,128)(2,1)}, u32[]{:S(2)}) copy-start(bf16[2,20,1280]{2,0,1:T(2,128)(2,1)} %param.8) | copy-start | bytes 307204
  596.1 25.8 %all-to-all-start.1 = ((bf16[128,2,200]{2,1,0:T(2,128)(2,1)}), bf16[128,2,200]{2,1,0:T(2,128)(2,1)S(1)}, u32[]{:S(2)}, u32[]{:S(2)}) async-start(bf16[128,2,200]{2,1,0:T(2,128)(2,1)} %reshape.210), calls=%async_computation.1 | async-start | bytes 262144 | tf_op jit(solution)/shard_map/all_to_all | solution.py:69
  626.1 8.8 %copy-start = (bf16[392,640]{1,0:T(8,128)(2,1)S(1)}, bf16[392,640]{1,0:T(8,128)(2,1)}, u32[]{:S(2)}) copy-start(bf16[392,640]{1,0:T(8,128)(2,1)} %param.9) | copy-start | bytes 1505284
  628.8 18.5 %all-to-all-start.2 = ((bf16[128,2,200]{2,1,0:T(2,128)(2,1)}), bf16[128,2,200]{2,1,0:T(2,128)(2,1)S(1)}, u32[]{:S(2)}, u32[]{:S(2)}) async-start(bf16[128,2,200]{2,1,0:T(2,128)(2,1)} %reshape.212), calls=%async_computation.2 | async-start | bytes 262144 | tf_op jit(solution)/shard_map/all_to_all | solution.py:76
Sparse Core Ops, SparseCore 0:
  14.7 207.1 all-reduce.1
  345.1 32.3 all-gather.1
